TPU v7x, 128 devices: a whole 4x4x4 slice. The times are simulated.
128 devices in a mesh: tok: 8 (over z, y_hi), head: 16 (over x, y_lo, core).
Axes of the slice: x: 4, y: 4 (y_hi: 2, y_lo: 2; y = y_hi * 2 + y_lo), z: 4, core: 2. Of those that a mesh axis runs over, the one named last changes fastest.
Arguments:
- states: bfloat16 [4096, 4096], P('tok', 'head'), may hold values from -400 to 400
- pre_gain: float32 [4096], replicated, may hold values from 0.5 to 1.5
- pre_shift: float32 [4096], replicated, may hold values from -1.75 to 1.75
- mlp_gain: float32 [4096], replicated, may hold values from 0.5 to 1.5
- mlp_shift: float32 [4096], replicated, may hold values from -1.75 to 1.75
- qkv_weight: bfloat16 [4096, 12288], P('tok', 'head'), may hold values from -0.09375 to 0.09375
- qkv_bias: float32 [12288], P('head'), may hold values from -1.75 to 1.75
- out_weight: bfloat16 [4096, 4096], P('head', 'tok'), may hold values from -0.125 to 0.125
- out_bias: float32 [4096], P('head'), may hold values from -1.75 to 1.75
- up_weight: bfloat16 [4096, 16384], P(None, 'head'), may hold values from -0.09375 to 0.09375
- up_bias: float32 [16384], P('head'), may hold values from -1.75 to 1.75
- down_weight: bfloat16 [16384, 4096], P('head'), may hold values from -0.0625 to 0.0625
- down_bias: float32 [4096], P('head'), may hold values from -1.75 to 1.75
- kv_cache: bfloat16 [1152, 2, 16, 4096], P(('tok', 'head')), may hold values from -320 to 320, as said below
- token_request: int32 [4096], P('tok'), may hold values from 0 to 15, as said below
- cached_len: int32 [16], P('tok'), may hold values from 128 to 1024, as said below
- page_table: int32 [16, 64], P('tok'), may hold values from 0 to 143, as said below
- migrations: int32 [64, 2], P('tok'), may hold values from 0 to 143, as said below
Outputs:
- update: bfloat16 [4096, 4096], P('tok', 'head')
Inputs may be any that keep to these rules, and one draw needn't show every extreme that they name: `token_request`: ids never fall; the tokens of request r lie among tokens (r // 2) * 512 to that plus 512 - 1, and every request has one token or more. `cached_len`: some request holds exactly 1024. `page_table`: the entries of one block are distinct. `migrations`: targets of one block are distinct and none is also a source of that block. `kv_cache`: keys are stored already rotated.
All inputs are finite; a program needn't handle non-finite values.
Results may differ from a plain program's by a relative error of at most 0.018.
The roundings to bfloat16 on the way count: a program that leaves them out, or rounds other values in their place, can miss the bound.
Values may be sent and summed in bfloat16 or wider, within the bound.
No kernel may reach another device: no remote copies, remote signals or barrier semaphores. Data moves between devices by JAX's collectives and lax.ppermute only.
A program may use at most 128 MiB of HBM per device.

v0:
```python
import jax
import jax.numpy as jnp
from jax import lax
from jax.sharding import PartitionSpec as P

HD = 128
ROT = 32
epsilon = 1e-05


def layer_norm(wide, gain, shift):
    row_mean = jnp.mean(wide, axis=1, keepdims=True)
    centred = wide - row_mean
    row_var = jnp.mean(centred * centred, axis=1, keepdims=True)
    return (centred * lax.rsqrt(row_var + epsilon) * gain + shift).astype(jnp.bfloat16)


def rotate(vectors, positions):
    half_rot = ROT // 2
    inv_freq = 10000.0 ** (-2.0 * jnp.arange(half_rot, dtype=jnp.float32) / ROT)
    angles = positions.astype(jnp.float32)[:, None] * inv_freq[None, :]
    cosine = jnp.cos(angles)[:, None, :]
    sine_part = jnp.sin(angles)[:, None, :]
    lower_half = vectors[..., :half_rot]
    upper_half = vectors[..., half_rot:ROT]
    return jnp.concatenate(
        [
            lower_half * cosine - upper_half * sine_part,
            upper_half * cosine + lower_half * sine_part,
            vectors[..., ROT:],
        ],
        axis=-1,
    )


def token_positions(local_req, cached):
    onehot = local_req[:, None] == jnp.arange(cached.shape[0], dtype=jnp.int32)[None, :]
    stretch_sizes = jnp.sum(onehot.astype(jnp.int32), axis=0)
    starts = jnp.cumsum(stretch_sizes) - stretch_sizes
    own_start = jnp.sum(jnp.where(onehot, starts[None, :], 0), axis=1)
    own_cached = jnp.sum(jnp.where(onehot, cached[None, :], 0), axis=1)
    return own_cached + jnp.arange(local_req.shape[0], dtype=jnp.int32) - own_start


def attend(queries, new_keys, new_values, cache_keys, cache_values, local_req, cached, positions):
    span = cache_keys.shape[0] // cached.shape[0]
    key_slot = jnp.arange(cache_keys.shape[0], dtype=jnp.int32)
    key_owner = key_slot // span
    key_place = key_slot % span
    cache_ok = (local_req[:, None] == key_owner[None, :]) & (
        key_place[None, :] < jnp.repeat(cached, span)[None, :]
    )
    new_ok = (local_req[:, None] == local_req[None, :]) & (positions[None, :] <= positions[:, None])
    allowed = jnp.concatenate([cache_ok, new_ok], axis=1)
    all_keys = jnp.concatenate([cache_keys, new_keys], axis=0)
    all_values = jnp.concatenate([cache_values, new_values], axis=0)
    scores = jnp.einsum(
        "thd,khd->htk", queries, all_keys, preferred_element_type=jnp.float32
    ) * HD ** (-0.5)
    scores = jnp.where(allowed[None], scores, -1e30)
    peak = jnp.max(scores, axis=2, keepdims=True)
    exp_scores = jnp.exp(scores - peak)
    attn_probs = (exp_scores / jnp.sum(exp_scores, axis=2, keepdims=True)).astype(jnp.bfloat16)
    return jnp.einsum(
        "htk,khd->thd", attn_probs, all_values, preferred_element_type=jnp.float32
    ).astype(jnp.bfloat16)


def share_pages(local_pool, groups):
    grouped = local_pool.reshape(
        local_pool.shape[0], 2, local_pool.shape[2], groups, local_pool.shape[3] // groups
    )
    shared = lax.all_to_all(grouped, "head", split_axis=3, concat_axis=0, tiled=True)
    return shared.reshape(shared.shape[0], 2, shared.shape[2], shared.shape[4])


def gather_by_all_to_all(block, axis):
    copies = jnp.concatenate([block] * lax.axis_size(axis), axis=0)
    return lax.all_to_all(copies, axis, split_axis=0, concat_axis=0, tiled=True)


def shards(
    states,
    pre_gain,
    pre_shift,
    mlp_gain,
    mlp_shift,
    qkv_weight,
    qkv_bias,
    out_weight,
    out_bias,
    up_weight,
    up_bias,
    down_weight,
    down_bias,
    kv_cache,
    token_request,
    cached_len,
    page_table,
    migrations,
):
    gathered = lax.all_gather(states, "head", axis=1, tiled=True)
    qkv_full = gather_by_all_to_all(qkv_weight, "tok")
    out_full = lax.all_gather(out_weight, "tok", axis=1, tiled=True)
    wide = gathered.astype(jnp.float32)
    pre_normed = layer_norm(wide, pre_gain, pre_shift)
    mlp_normed = layer_norm(wide, mlp_gain, mlp_shift)
    tok_rows = gathered.shape[0]
    half = tok_rows // 2

    def feed(normed):
        hidden = jax.nn.gelu(
            jnp.dot(normed, up_weight, preferred_element_type=jnp.float32) + up_bias,
            approximate=False,
        ).astype(jnp.bfloat16)
        return jnp.dot(hidden, down_weight, preferred_element_type=jnp.float32)

    feed_first = feed(mlp_normed[:half])
    kv_cache, feed_first = lax.optimization_barrier((kv_cache, feed_first))
    page_pool = share_pages(kv_cache, lax.axis_size("head"))
    joined = jnp.dot(pre_normed, qkv_full, preferred_element_type=jnp.float32)
    joined = (joined + qkv_bias).reshape(tok_rows, -1, 3, HD)
    local_req = token_request - lax.axis_index("tok") * cached_len.shape[0]
    positions = token_positions(local_req, cached_len)
    queries = rotate(joined[:, :, 0], positions).astype(jnp.bfloat16)
    new_keys = rotate(joined[:, :, 1], positions).astype(jnp.bfloat16)
    new_values = joined[:, :, 2].astype(jnp.bfloat16)
    sources = migrations[:, 0]
    targets = migrations[:, 1]
    table = page_table.reshape(-1)
    match = table[:, None] == targets[None, :]
    moved_from = jnp.sum(jnp.where(match, sources[None, :], 0), axis=1)
    table = jnp.where(jnp.any(match, axis=1), moved_from, table)
    pages = page_pool[table]
    cache_keys = pages[:, 0].reshape(-1, queries.shape[1], HD)
    cache_values = pages[:, 1].reshape(-1, queries.shape[1], HD)
    heads_out = attend(
        queries, new_keys, new_values, cache_keys, cache_values, local_req, cached_len, positions
    ).reshape(tok_rows, -1)
    attention_part = jnp.dot(heads_out, out_full, preferred_element_type=jnp.float32)
    both_first = (attention_part[:half] + feed_first).astype(jnp.bfloat16)
    both_first, normed_second = lax.optimization_barrier((both_first, mlp_normed[half:]))
    summed_first = lax.psum_scatter(both_first, "head", scatter_dimension=1, tiled=True)
    both_second = (attention_part[half:] + feed(normed_second)).astype(jnp.bfloat16)
    summed_second = lax.psum_scatter(both_second, "head", scatter_dimension=1, tiled=True)
    summed = jnp.concatenate([summed_first, summed_second], axis=0).astype(jnp.float32)
    return (summed + out_bias + down_bias).astype(jnp.bfloat16)


def solution(mesh):
    in_specs = (
        P("tok", "head"),
        P(),
        P(),
        P(),
        P(),
        P("tok", "head"),
        P("head"),
        P("head", "tok"),
        P("head"),
        P(None, "head"),
        P("head"),
        P("head", None),
        P("head"),
        P(("tok", "head"), None, None, None),
        P("tok"),
        P("tok"),
        P("tok", None),
        P("tok", None),
    )
    out_specs = P("tok", "head")
    return jax.shard_map(shards, mesh=mesh, in_specs=in_specs, out_specs=out_specs, check_vma=False)
```

profile of v0, /device:TPU:0, one launch (start us, length us, event | category | flops | bytes accessed | tf_op | source)
XLA Modules:
  0.0 333.2 jit_solution(9796448847202854535)
XLA Ops:
  7.3 1.2 constant_dynamic-update-slice_fusion.7
  8.4 1.2 constant_dynamic-update-slice_fusion.6
  9.6 1.2 constant_dynamic-update-slice_fusion.5
  10.8 1.2 constant_dynamic-update-slice_fusion.4
  12.3 2.6 copy-done.3
  14.9 8.2 %all-to-all-start.1 = ((bf16[8,512,768]{2,1,0:T(8,128)(2,1)}), bf16[8,512,768]{2,1,0:T(8,128)(2,1)}, u32[]{:S(2)}, u32[]{:S(2)}) async-start(bf16[8,512,768]{2,1,0:T(8,128)(2,1)} %bitcast.55), calls=%async_computation.1 | async-start | bytes 12582912 | tf_op jit(solution)/shard_map/all_to_all | solution.py:79
  28.8 35.1 %all-gather.3.cloned.1.call-done = bf16[512,4096]{1,0:T(8,128)(2,1)} async-done(((bf16[512,256]{1,0:T(8,128)(2,1)}), bf16[512,4096]{1,0:T(8,128)(2,1)}) %all-gather.3.cloned.1.call-update) | async-done | bytes 4194320 | tf_op jit(solution)/shard_map/all_gather | solution.py:102
  63.9 3.0 convert_reduce_fusion
  67.4 1.2 fusion.9
  68.6 3.6 %fusion.6 = bf16[512,4096]{1,0:T(8,128)(2,1)} fusion(bf16[512,4096]{1,0:T(8,128)(2,1)S(1)} %copy-done.1, f32[4096]{0:T(1024)S(1)} %copy-done.8, f32[4096]{0:T(1024)S(1)} %copy-done.9, f32[512]{0:T(512)S(1)} %add_rsqrt_fusion, f32[512]{0:T(512)S(1)} %broadcast_multiply_fusion), kind=kLoop, calls=%fused_computation.12 | loop fusion | flops 12582912 | bytes 8425472 | tf_op jit(solution)/shard_map/convert_element_type | solution.py:15
  72.2 15.4 %fusion.68 = f32[256,4096]{1,0:T(8,128)} fusion(bf16[1024,4096]{1,0:T(8,128)(2,1)} %param.29, bf16[4096,1024]{1,0:T(8,128)(2,1)} %param.27, bf16[512,4096]{1,0:T(8,128)(2,1)} %fusion.6, f32[1024]{0:T(1024)S(1)} %copy-done.18), kind=kOutput, calls=%fused_computation.89 | convolution fusion | flops 4312268800 | bytes 23072768 | tf_op jit(solution)/shard_map/dot_general | solution.py:116
  87.6 1.8 copy.68
  89.4 27.1 %all-to-all-done.1 = bf16[8,512,768]{2,1,0:T(8,128)(2,1)} async-done(((bf16[8,512,768]{2,1,0:T(8,128)(2,1)}), bf16[8,512,768]{2,1,0:T(8,128)(2,1)}, u32[]{:S(2)}, u32[]{:S(2)}) %all-to-all-start.1) | async-done | bytes 6291488 | tf_op jit(solution)/shard_map/all_to_all | solution.py:79
  116.5 4.1 %all-to-all-start = ((bf16[9,2,16,16,256]{4,2,1,0,3:T(8,128)(2,1)}), bf16[9,2,16,16,256]{4,2,1,0,3:T(8,128)(2,1)S(1)}, u32[]{:S(2)}, u32[]{:S(2)}) async-start(bf16[9,2,16,16,256]{4,2,1,0,3:T(8,128)(2,1)} %bitcast.53), calls=%async_computation | async-start | bytes 4718592 | tf_op jit(solution)/shard_map/all_to_all | solution.py:73
  120.9 9.1 %fusion.25 = f32[512,768]{1,0:T(8,128)} fusion(bf16[4096,768]{1,0:T(8,128)(2,1)} %bitcast.9, bf16[512,4096]{1,0:T(8,128)(2,1)} %all-gather.3.cloned.1.call-done, f32[4096]{0:T(1024)S(1)} %copy-done.15, f32[4096]{0:T(1024)S(1)} %copy-done.16, f32[512]{0:T(512)S(1)} %add_rsqrt_fusion, f32[512]{0:T(512)S(1)} %broadcast_multiply_fusion, f32[768]{0:T(1024)S(1)} %copy-done.17), kind=kOutput, calls=%fused_computation.37 | convolution fusion | flops 3234201600 | bytes 12098560 | tf_op jit(solution)/shard_map/dot_general | solution.py:121
  130.0 3.1 copy.50
  133.1 2.1 fusion.217
  135.4 1.2 copy.59
  138.3 1.8 fusion.136
  140.1 2.5 subtract_convert_fusion.1
  142.5 8.7 %all-to-all-done = bf16[9,2,16,16,256]{4,2,1,0,3:T(8,128)(2,1)S(1)} async-done(((bf16[9,2,16,16,256]{4,2,1,0,3:T(8,128)(2,1)}), bf16[9,2,16,16,256]{4,2,1,0,3:T(8,128)(2,1)S(1)}, u32[]{:S(2)}, u32[]{:S(2)}) %all-to-all-start) | async-done | bytes 2359328 | tf_op jit(solution)/shard_map/all_to_all | solution.py:73
  151.2 2.0 gather_fusion
  153.2 1.7 fusion.216
  157.5 10.2 %fusion.218 = (f32[2,512]{1,0:T(2,128)S(1)}, f32[2,512,2560]{2,1,0:T(8,128)}) fusion(pred[512,2560]{1,0:T(8,128)(4,1)S(1)} %copy-done.6, bf16[512,2,96]{2,0,1:T(8,128)(2,1)} %slice.112, bf16[512,2,16]{2,0,1:T(8,128)(2,1)} %get-tuple-element.25, bf16[512,2,16]{2,0,1:T(8,128)(2,1)} %get-tuple-element.26, bf16[2048,2,128]{2,0,1:T(8,128)(2,1)} %copy.57, ...), kind=kOutput, calls=%fused_computation.272 | convolution fusion | flops 687606272 | bytes 13373440 | tf_op jit(solution)/shard_map/sub | solution.py:62
  167.7 5.9 %fusion.42 = bf16[2,128,512]{2,1,0:T(8,128)(2,1)S(1)} fusion(f32[2,512,2560]{2,1,0:T(8,128)} %get-tuple-element.32, f32[2,512]{1,0:T(2,128)S(1)} %get-tuple-element.31, bf16[512,2,128]{0,2,1:T(8,128)(2,1)S(1)} %copy-done.7, bf16[2048,2,128]{0,2,1:T(8,128)(2,1)S(1)} %copy.52), kind=kOutput, calls=%fused_computation.51 | convolution fusion | flops 679084032 | bytes 12062720 | tf_op jit(solution)/shard_map/htk,khd->thd/dot_general | solution.py:64
  173.6 3.0 fusion.221
  176.6 3.2 copy-done.2
  179.9 1.9 fusion.18
  181.7 15.1 %fusion.15 = bf16[256,4096]{1,0:T(8,128)(2,1)} fusion(bf16[1024,4096]{1,0:T(8,128)(2,1)} %param.29, f32[512,4096]{1,0:T(8,128)} %copy-done.2, bf16[256,4096]{1,0:T(8,128)(2,1)S(1)} %slice-done, bf16[4096,1024]{1,0:T(8,128)(2,1)} %param.27, f32[1024]{0:T(1024)S(1)} %copy-done.18), kind=kOutput, calls=%fused_computation.23 | convolution fusion | flops 4314365952 | bytes 25169920 | tf_op jit(solution)/shard_map/dot_general | solution.py:116
  197.4 62.5 %reduce-scatter.5.cloned.1.call-done = bf16[256,256]{1,0:T(8,128)(2,1)} async-done(((bf16[256,4096]{1,0:T(8,128)(2,1)}), bf16[256,256]{1,0:T(8,128)(2,1)}) %reduce-scatter.5.cloned.1.call-update) | async-done | bytes 131088 | tf_op jit(solution)/shard_map/reduce_scatter | solution.py:145
  260.0 64.9 %reduce-scatter.3.cloned.1.call-done = bf16[256,256]{1,0:T(8,128)(2,1)} async-done(((bf16[256,4096]{1,0:T(8,128)(2,1)}), bf16[256,256]{1,0:T(8,128)(2,1)}) %reduce-scatter.3.cloned.1.call-update) | async-done | bytes 131088 | tf_op jit(solution)/shard_map/reduce_scatter | solution.py:143
  324.9 1.7 add_convert_fusion
  (85 shorter events, 12.3 us)
Async XLA Ops:
  6.5 5.5 %copy-start = (bf16[512,768]{1,0:T(8,128)(2,1)S(1)}, bf16[512,768]{1,0:T(8,128)(2,1)}, u32[]{:S(2)}) copy-start(bf16[512,768]{1,0:T(8,128)(2,1)} %param.23) | copy-start | bytes 2359300
  6.5 57.4 %all-gather.3.cloned.1.call-start = ((), (), s32[]{:S(2)}) async-start(), calls=%async_computation.4 | async-start | bytes 4456448 | tf_op jit(solution)/shard_map/all_gather | solution.py:102
  12.3 2.7 copy-start.3
  14.9 9.0 %copy-start.19 = (s32[2,64]{1,0:T(2,128)S(1)}, s32[2,64]{1,0:T(2,128)}, u32[]{:S(2)}) copy-start(s32[2,64]{1,0:T(2,128)} %param.34) | copy-start | bytes 1540
  14.9 9.1 %copy-start.11 = (s32[512]{0:T(512)S(1)}, s32[512]{0:T(512)}, u32[]{:S(2)}) copy-start(s32[512]{0:T(512)} %param.32) | copy-start | bytes 6148
  14.9 9.4 %copy-start.10 = (s32[2]{0:T(128)S(1)}, s32[2]{0:T(128)}, u32[]{:S(2)}) copy-start(s32[2]{0:T(128)} %param.33) | copy-start | bytes 28
  14.9 11.5 %copy-start.14 = (s32[8,2]{0,1:T(2,128)S(1)}, s32[8,2]{0,1:T(2,128)}, u32[]{:S(2)}) copy-start(s32[8,2]{0,1:T(2,128)} %param.35) | copy-start | bytes 196
  14.9 101.6 %all-to-all-start.1 = ((bf16[8,512,768]{2,1,0:T(8,128)(2,1)}), bf16[8,512,768]{2,1,0:T(8,128)(2,1)}, u32[]{:S(2)}, u32[]{:S(2)}) async-start(bf16[8,512,768]{2,1,0:T(8,128)(2,1)} %bitcast.55), calls=%async_computation.1 | async-start | bytes 12582912 | tf_op jit(solution)/shard_map/all_to_all | solution.py:79
  23.1 150.5 %all-gather.5.cloned.1.call-start = ((), (), s32[]{:S(2)}) async-start(), calls=%async_computation.5 | async-start | bytes 2359296 | tf_op jit(solution)/shard_map/all_gather | solution.py:104
  25.6 43.0 %copy-start.8 = (f32[4096]{0:T(1024)S(1)}, f32[4096]{0:T(1024)}, u32[]{:S(2)}) copy-start(f32[4096]{0:T(1024)} %param.22) | copy-start | bytes 49156
  25.6 43.0 %copy-start.9 = (f32[4096]{0:T(1024)S(1)}, f32[4096]{0:T(1024)}, u32[]{:S(2)}) copy-start(f32[4096]{0:T(1024)} %param.21) | copy-start | bytes 49156
  63.9 3.4 %copy-start.1 = (bf16[512,4096]{1,0:T(8,128)(2,1)S(1)}, bf16[512,4096]{1,0:T(8,128)(2,1)}, u32[]{:S(2)}) copy-start(bf16[512,4096]{1,0:T(8,128)(2,1)} %all-gather.3.cloned.1.call-done) | copy-start | bytes 12582916
  67.4 4.8 %copy-start.18 = (f32[1024]{0:T(1024)S(1)}, f32[1024]{0:T(1024)}, u32[]{:S(2)}) copy-start(f32[1024]{0:T(1024)} %param.28) | copy-start | bytes 12292
  72.2 15.4 %copy-start.5 = (bf16[9,2,16,4096]{3,2,1,0:T(8,128)(2,1)S(1)}, bf16[9,2,16,4096]{3,2,1,0:T(8,128)(2,1)}, u32[]{:S(2)}) copy-start(bf16[9,2,16,4096]{3,2,1,0:T(8,128)(2,1)} %param.31) | copy-start | bytes 7077892
  87.6 33.3 %copy-start.15 = (f32[4096]{0:T(1024)S(1)}, f32[4096]{0:T(1024)}, u32[]{:S(2)}) copy-start(f32[4096]{0:T(1024)} %param.20) | copy-start | bytes 49156
  87.6 33.3 %copy-start.16 = (f32[4096]{0:T(1024)S(1)}, f32[4096]{0:T(1024)}, u32[]{:S(2)}) copy-start(f32[4096]{0:T(1024)} %param.19) | copy-start | bytes 49156
  87.6 33.3 %copy-start.17 = (f32[768]{0:T(1024)S(1)}, f32[768]{0:T(1024)}, u32[]{:S(2)}) copy-start(f32[768]{0:T(1024)} %param.24) | copy-start | bytes 9220
  116.5 34.7 %all-to-all-start = ((bf16[9,2,16,16,256]{4,2,1,0,3:T(8,128)(2,1)}), bf16[9,2,16,16,256]{4,2,1,0,3:T(8,128)(2,1)S(1)}, u32[]{:S(2)}, u32[]{:S(2)}) async-start(bf16[9,2,16,16,256]{4,2,1,0,3:T(8,128)(2,1)} %bitcast.53), calls=%async_computation | async-start | bytes 4718592 | tf_op jit(solution)/shard_map/all_to_all | solution.py:73
  120.6 139.4 %reduce-scatter.5.cloned.1.call-start = ((), (), s32[]{:S(2)}) async-start(), calls=%async_computation.7 | async-start | bytes 2228224 | tf_op jit(solution)/shard_map/reduce_scatter | solution.py:145
  155.2 2.2 copy-start.6
  157.5 10.2 %copy-start.7 = (bf16[512,2,128]{0,2,1:T(8,128)(2,1)S(1)}, bf16[512,2,128]{0,2,1:T(8,128)(2,1)}, u32[]{:S(2)}) copy-start(bf16[512,2,128]{0,2,1:T(8,128)(2,1)} %fusion.136) | copy-start | bytes 786436
  173.6 6.3 %copy-start.4 = (f32[256,4096]{1,0:T(8,128)S(1)}, f32[256,4096]{1,0:T(8,128)}, u32[]{:S(2)}) copy-start(f32[256,4096]{1,0:T(8,128)} %fusion.68) | copy-start | bytes 12582916
  176.6 3.2 copy-start.2
  179.9 1.9 slice-start
  181.7 143.1 %copy-start.12 = (f32[256]{0:T(256)S(1)}, f32[256]{0:T(256)}, u32[]{:S(2)}) copy-start(f32[256]{0:T(256)} %param.30) | copy-start | bytes 3076
  181.7 143.1 %copy-start.13 = (f32[256]{0:T(256)S(1)}, f32[256]{0:T(256)}, u32[]{:S(2)}) copy-start(f32[256]{0:T(256)} %param.26) | copy-start | bytes 3076
  196.9 128.0 %reduce-scatter.3.cloned.1.call-start = ((), (), s32[]{:S(2)}) async-start(), calls=%async_computation.6 | async-start | bytes 2228224 | tf_op jit(solution)/shard_map/reduce_scatter | solution.py:143
Sparse Core Ops, SparseCore 0:
  9.0 54.9 all-gather.2
  66.1 83.3 all-gather.4
  197.0 62.9 reduce-scatter.4
  262.2 62.6 reduce-scatter.2
where the time goes:
time: 334 us; the launch traced here: 333 us
  waiting for transfers between devices  200 us (60%)
  matrix products  58.7 us (18%)
  local copies, waits for them, and re-layouts  31.3 us (9%)
  other arithmetic  16.8 us (5%)
  between operations  13.4 us (4%)
  starting transfers between devices  12.6 us (4%)
    reduce_scatter x1, waiting for transfers between devices, shards(): lax.psum_scatter(both_first, 'head', scatter_dimension=1, tiled=True)  64.9 us
    reduce_scatter x1, waiting for transfers between devices, shards(): lax.psum_scatter(both_second, 'head', scatter_dimension=1, tiled=True)  62.5 us
    all_gather x1, waiting for transfers between devices, shards(): gathered = lax.all_gather(states, 'head', axis=1, tiled=True)  35.1 us
    dot_general x2, matrix products, feed(): return jnp.dot(hidden, down_weight, preferred_element_type=jnp.float32)  30.5 us
    all_to_all x1, waiting for transfers between devices, gather_by_all_to_all(): return lax.all_to_all(copies, axis, split_axis=0, concat_axis=0, tiled=True)  27.1 us
    unnamed x50, local copies, waits for them, and re-layouts  12.8 us
    sub x1, matrix products, attend(): exp_scores = jnp.exp(scores - peak)  10.2 us
    dot_general x1, matrix products, shards(): joined = jnp.dot(pre_normed, qkv_full, preferred_element_type=jnp.float32)  9.12 us
  transfers between devices with their start and end apart: 6, of which 5 were waited for; matrix products, arithmetic and copies ran while one was open for 24% of the time, Pallas kernels for 0%

commit v1 on v0

--- a/solution.py
+++ b/solution.py
@@ -99,7 +99,9 @@
     page_table,
     migrations,
 ):
-    gathered = lax.all_gather(states, "head", axis=1, tiled=True)
+    gathered = jnp.concatenate(
+        lax.all_to_all(jnp.stack([states] * lax.axis_size("head")), "head", 0, 0), axis=1
+    )
     qkv_full = gather_by_all_to_all(qkv_weight, "tok")
     out_full = lax.all_gather(out_weight, "tok", axis=1, tiled=True)
     wide = gathered.astype(jnp.float32)

time: 334 us -> 384 us (1.15)
  waiting for transfers between devices: 200 us -> 237 us
  starting transfers between devices: 12.6 us -> 23.8 us
  other arithmetic: 16.8 us -> 23.1 us
    all_to_all x0 -> x1, waiting for transfers between devices: none -> 47.7 us  [shards(): lax.all_to_all(jnp.stack([states] * lax.axis_size('head')), 'head', 0, 0)]
    all_gather x1 -> x0, waiting for transfers between devices: 35.1 us -> none  [shards(): gathered = lax.all_gather(states, 'head', axis=1, tiled=True)]
    all_to_all x1, waiting for transfers between devices: 27.1 us -> 53.9 us  [gather_by_all_to_all(): return lax.all_to_all(copies, axis, split_axis=0, concat_axis=0, tiled=True)]
    all_to_all x1, starting transfers between devices: 4.08 us -> 10.2 us  [share_pages(): lax.all_to_all(grouped, 'head', split_axis=3, concat_axis=0, tiled=True)]
    all_to_all x0 -> x1, starting transfers between devices: none -> 5.69 us  [shards(): lax.all_to_all(jnp.stack([states] * lax.axis_size('head')), 'head', 0, 0)]
    convert_element_type x1 -> x2, other arithmetic: 3.55 us -> 7.7 us  [layer_norm(): (centred * lax.rsqrt(row_var + epsilon) * gain + shift).astype(jnp.bfloat16)]
    unnamed x50 -> x49, local copies, waits for them, and re-layouts: 12.8 us -> 8.88 us
  transfers between devices with their start and end apart: 6 -> 6, of which waited for: 5 -> 5; matrix products, arithmetic and copies ran while one was open for 24% -> 20% of each run, Pallas kernels for 0% -> 0%
where the time goes in v1:
time: 384 us
  waiting for transfers between devices  237 us (62%)
  matrix products  56.4 us (15%)
  local copies, waits for them, and re-layouts  29.7 us (8%)
  starting transfers between devices  23.8 us (6%)
  other arithmetic  23.1 us (6%)
  between operations  13.5 us (4%)
    reduce_scatter x1, waiting for transfers between devices, shards(): lax.psum_scatter(both_first, 'head', scatter_dimension=1, tiled=True)  64.8 us
    reduce_scatter x1, waiting for transfers between devices, shards(): lax.psum_scatter(both_second, 'head', scatter_dimension=1, tiled=True)  61.5 us
    all_to_all x1, waiting for transfers between devices, gather_by_all_to_all(): return lax.all_to_all(copies, axis, split_axis=0, concat_axis=0, tiled=True)  53.9 us
    all_to_all x1, waiting for transfers between devices, shards(): lax.all_to_all(jnp.stack([states] * lax.axis_size('head')), 'head', 0, 0)  47.7 us
    dot_general x2, matrix products, feed(): return jnp.dot(hidden, down_weight, preferred_element_type=jnp.float32)  30.4 us
    all_to_all x1, starting transfers between devices, share_pages(): lax.all_to_all(grouped, 'head', split_axis=3, concat_axis=0, tiled=True)  10.2 us
    sub x1, matrix products, attend(): exp_scores = jnp.exp(scores - peak)  10.2 us
    unnamed x49, local copies, waits for them, and re-layouts  8.88 us
  transfers between devices with their start and end apart: 6, of which 5 were waited for; matrix products, arithmetic and copies ran while one was open for 20% of the time, Pallas kernels for 0%

profile of v1, /device:TPU:0, one launch (start us, length us, event | category | flops | bytes accessed | tf_op | source)
XLA Modules:
  0.0 383.6 jit_solution(17580532539073541072)
XLA Ops:
  7.6 2.3 stack.2
  10.0 5.7 %all-to-all-start = ((bf16[16,512,256]{1,2,0:T(8,128)(2,1)}), bf16[16,512,256]{1,2,0:T(8,128)(2,1)}, u32[]{:S(2)}, u32[]{:S(2)}) async-start(bf16[16,512,256]{1,2,0:T(8,128)(2,1)} %stack.2), calls=%async_computation | async-start | bytes 8388608 | tf_op jit(solution)/shard_map/all_to_all | solution.py:103
  17.7 2.6 copy-done.2
  20.6 47.7 %all-to-all-done = bf16[16,512,256]{1,2,0:T(8,128)(2,1)} async-done(((bf16[16,512,256]{1,2,0:T(8,128)(2,1)}), bf16[16,512,256]{1,2,0:T(8,128)(2,1)}, u32[]{:S(2)}, u32[]{:S(2)}) %all-to-all-start) | async-done | bytes 4194336 | tf_op jit(solution)/shard_map/all_to_all | solution.py:103
  68.3 7.8 %all-to-all-start.2 = ((bf16[8,512,768]{2,1,0:T(8,128)(2,1)}), bf16[8,512,768]{2,1,0:T(8,128)(2,1)}, u32[]{:S(2)}, u32[]{:S(2)}) async-start(bf16[8,512,768]{2,1,0:T(8,128)(2,1)} %bitcast.71), calls=%async_computation.2 | async-start | bytes 12582912 | tf_op jit(solution)/shard_map/all_to_all | solution.py:79
  78.9 1.2 pad_add_fusion
  80.0 2.8 convert_reduce_fusion
  82.9 3.5 multiply_reduce_fusion
  86.4 4.5 %fusion.4 = bf16[512,4096]{0,1:T(8,128)(2,1)} fusion(bf16[16,512,256]{1,2,0:T(8,128)(2,1)} %all-to-all-done, f32[4096]{0:T(1024)S(1)} %copy-done.7, f32[4096]{0:T(1024)S(1)} %copy-done.8, f32[512]{0:T(512)S(1)} %add_rsqrt_fusion, f32[512]{0:T(512)S(1)} %broadcast_multiply_fusion), kind=kLoop, calls=%fused_computation.9 | loop fusion | flops 12582912 | bytes 8425472 | tf_op jit(solution)/shard_map/convert_element_type | solution.py:15
  90.9 15.3 %fusion.54 = f32[256,4096]{1,0:T(8,128)} fusion(bf16[1024,4096]{1,0:T(8,128)(2,1)} %param.29, bf16[4096,1024]{1,0:T(8,128)(2,1)} %param.27, bf16[512,4096]{0,1:T(8,128)(2,1)} %fusion.4, f32[1024]{0:T(1024)S(1)} %copy-done.17), kind=kOutput, calls=%fused_computation.81 | convolution fusion | flops 4312268800 | bytes 23072768 | tf_op jit(solution)/shard_map/dot_general | solution.py:118
  106.2 1.8 copy.73
  108.0 53.9 %all-to-all-done.2 = bf16[8,512,768]{2,1,0:T(8,128)(2,1)} async-done(((bf16[8,512,768]{2,1,0:T(8,128)(2,1)}), bf16[8,512,768]{2,1,0:T(8,128)(2,1)}, u32[]{:S(2)}, u32[]{:S(2)}) %all-to-all-start.2) | async-done | bytes 6291488 | tf_op jit(solution)/shard_map/all_to_all | solution.py:79
  161.8 10.2 %all-to-all-start.1 = ((bf16[9,2,16,16,256]{4,2,1,0,3:T(8,128)(2,1)}), bf16[9,2,16,16,256]{4,2,1,0,3:T(8,128)(2,1)S(1)}, u32[]{:S(2)}, u32[]{:S(2)}) async-start(bf16[9,2,16,16,256]{4,2,1,0,3:T(8,128)(2,1)} %bitcast.69), calls=%async_computation.1 | async-start | bytes 4718592 | tf_op jit(solution)/shard_map/all_to_all | solution.py:73
  172.1 3.2 add_convert_fusion
  175.4 6.9 %convolution_add_fusion.1 = f32[512,768]{1,0:T(8,128)} fusion(bf16[512,4096]{0,1:T(8,128)(2,1)S(1)} %bitcast.78, bf16[4096,768]{1,0:T(8,128)(2,1)} %bitcast.13, f32[768]{0:T(1024)S(1)} %copy-done.16), kind=kOutput, calls=%fused_computation.29 | convolution fusion | flops 3221618688 | bytes 12061696 | tf_op jit(solution)/shard_map/dot_general | solution.py:123
  182.3 3.0 copy.55
  185.3 2.1 fusion.203
  187.6 1.2 copy.64
  190.5 1.8 fusion.122
  192.3 2.5 subtract_convert_fusion.1
  194.8 7.9 %all-to-all-done.1 = bf16[9,2,16,16,256]{4,2,1,0,3:T(8,128)(2,1)S(1)} async-done(((bf16[9,2,16,16,256]{4,2,1,0,3:T(8,128)(2,1)}), bf16[9,2,16,16,256]{4,2,1,0,3:T(8,128)(2,1)S(1)}, u32[]{:S(2)}, u32[]{:S(2)}) %all-to-all-start.1) | async-done | bytes 2359328 | tf_op jit(solution)/shard_map/all_to_all | solution.py:73
  202.6 2.0 gather_fusion
  204.6 1.7 fusion.202
  208.9 10.2 %fusion.204 = (f32[2,512]{1,0:T(2,128)S(1)}, f32[2,512,2560]{2,1,0:T(8,128)}) fusion(pred[512,2560]{1,0:T(8,128)(4,1)S(1)} %copy-done.5, bf16[512,2,96]{2,0,1:T(8,128)(2,1)} %slice.112, bf16[512,2,16]{2,0,1:T(8,128)(2,1)} %get-tuple-element.25, bf16[512,2,16]{2,0,1:T(8,128)(2,1)} %get-tuple-element.26, bf16[2048,2,128]{2,0,1:T(8,128)(2,1)} %copy.62, ...), kind=kOutput, calls=%fused_computation.264 | convolution fusion | flops 687606272 | bytes 13373440 | tf_op jit(solution)/shard_map/sub | solution.py:62
  219.1 5.9 %fusion.28 = bf16[2,128,512]{2,1,0:T(8,128)(2,1)S(1)} fusion(f32[2,512,2560]{2,1,0:T(8,128)} %get-tuple-element.32, f32[2,512]{1,0:T(2,128)S(1)} %get-tuple-element.31, bf16[512,2,128]{0,2,1:T(8,128)(2,1)S(1)} %copy-done.6, bf16[2048,2,128]{0,2,1:T(8,128)(2,1)S(1)} %copy.57), kind=kOutput, calls=%fused_computation.43 | convolution fusion | flops 679084032 | bytes 12062720 | tf_op jit(solution)/shard_map/htk,khd->thd/dot_general | solution.py:64
  225.0 3.0 fusion.207
  228.1 3.2 copy-done.1
  231.3 1.9 fusion.11
  233.2 15.1 %fusion.10 = bf16[256,4096]{1,0:T(8,128)(2,1)} fusion(bf16[1024,4096]{1,0:T(8,128)(2,1)} %param.29, f32[512,4096]{1,0:T(8,128)} %copy-done.1, bf16[256,4096]{0,1:T(8,128)(2,1)S(1)} %slice-done, bf16[4096,1024]{1,0:T(8,128)(2,1)} %param.27, f32[1024]{0:T(1024)S(1)} %copy-done.17), kind=kOutput, calls=%fused_computation.20 | convolution fusion | flops 4314365952 | bytes 25169920 | tf_op jit(solution)/shard_map/dot_general | solution.py:118
  249.0 61.5 %reduce-scatter.5.cloned.1.call-done = bf16[256,256]{1,0:T(8,128)(2,1)} async-done(((bf16[256,4096]{1,0:T(8,128)(2,1)}), bf16[256,256]{1,0:T(8,128)(2,1)}) %reduce-scatter.5.cloned.1.call-update) | async-done | bytes 131088 | tf_op jit(solution)/shard_map/reduce_scatter | solution.py:147
  310.5 64.8 %reduce-scatter.3.cloned.1.call-done = bf16[256,256]{1,0:T(8,128)(2,1)} async-done(((bf16[256,4096]{1,0:T(8,128)(2,1)}), bf16[256,256]{1,0:T(8,128)(2,1)}) %reduce-scatter.3.cloned.1.call-update) | async-done | bytes 131088 | tf_op jit(solution)/shard_map/reduce_scatter | solution.py:145
  375.3 1.7 add_convert_fusion.1
  (87 shorter events, 11.2 us)
Async XLA Ops:
  10.0 6.5 %copy-start.18 = (s32[2,64]{1,0:T(2,128)S(1)}, s32[2,64]{1,0:T(2,128)}, u32[]{:S(2)}) copy-start(s32[2,64]{1,0:T(2,128)} %param.34) | copy-start | bytes 1540
  10.0 6.6 %copy-start.12 = (s32[512]{0:T(512)S(1)}, s32[512]{0:T(512)}, u32[]{:S(2)}) copy-start(s32[512]{0:T(512)} %param.32) | copy-start | bytes 6148
  10.0 7.0 %copy-start.15 = (s32[8,2]{0,1:T(2,128)S(1)}, s32[8,2]{0,1:T(2,128)}, u32[]{:S(2)}) copy-start(s32[8,2]{0,1:T(2,128)} %param.35) | copy-start | bytes 196
  10.0 7.2 %copy-start.11 = (s32[2]{0:T(128)S(1)}, s32[2]{0:T(128)}, u32[]{:S(2)}) copy-start(s32[2]{0:T(128)} %param.33) | copy-start | bytes 28
  10.0 7.2 %copy-start = (bf16[512,768]{1,0:T(8,128)(2,1)S(1)}, bf16[512,768]{1,0:T(8,128)(2,1)}, u32[]{:S(2)}) copy-start(bf16[512,768]{1,0:T(8,128)(2,1)} %param.23) | copy-start | bytes 2359300
  10.0 58.3 %all-to-all-start = ((bf16[16,512,256]{1,2,0:T(8,128)(2,1)}), bf16[16,512,256]{1,2,0:T(8,128)(2,1)}, u32[]{:S(2)}, u32[]{:S(2)}) async-start(bf16[16,512,256]{1,2,0:T(8,128)(2,1)} %stack.2), calls=%async_computation | async-start | bytes 8388608 | tf_op jit(solution)/shard_map/all_to_all | solution.py:103
  15.7 209.3 %all-gather.2.cloned.1.call-start = ((), (), s32[]{:S(2)}) async-start(), calls=%async_computation.5 | async-start | bytes 2359296 | tf_op jit(solution)/shard_map/all_gather | solution.py:106
  17.7 2.6 copy-start.2
  68.3 9.5 %copy-start.9 = (f32[4096]{0:T(1024)S(1)}, f32[4096]{0:T(1024)}, u32[]{:S(2)}) copy-start(f32[4096]{0:T(1024)} %param.20) | copy-start | bytes 49156
  68.3 9.5 %copy-start.10 = (f32[4096]{0:T(1024)S(1)}, f32[4096]{0:T(1024)}, u32[]{:S(2)}) copy-start(f32[4096]{0:T(1024)} %param.19) | copy-start | bytes 49156
  68.3 93.5 %all-to-all-start.2 = ((bf16[8,512,768]{2,1,0:T(8,128)(2,1)}), bf16[8,512,768]{2,1,0:T(8,128)(2,1)}, u32[]{:S(2)}, u32[]{:S(2)}) async-start(bf16[8,512,768]{2,1,0:T(8,128)(2,1)} %bitcast.71), calls=%async_computation.2 | async-start | bytes 12582912 | tf_op jit(solution)/shard_map/all_to_all | solution.py:79
  78.9 7.5 %copy-start.7 = (f32[4096]{0:T(1024)S(1)}, f32[4096]{0:T(1024)}, u32[]{:S(2)}) copy-start(f32[4096]{0:T(1024)} %param.22) | copy-start | bytes 49156
  78.9 7.5 %copy-start.8 = (f32[4096]{0:T(1024)S(1)}, f32[4096]{0:T(1024)}, u32[]{:S(2)}) copy-start(f32[4096]{0:T(1024)} %param.21) | copy-start | bytes 49156
  86.3 4.5 %copy-start.17 = (f32[1024]{0:T(1024)S(1)}, f32[1024]{0:T(1024)}, u32[]{:S(2)}) copy-start(f32[1024]{0:T(1024)} %param.28) | copy-start | bytes 12292
  90.9 15.3 %copy-start.4 = (bf16[9,2,16,4096]{3,2,1,0:T(8,128)(2,1)S(1)}, bf16[9,2,16,4096]{3,2,1,0:T(8,128)(2,1)}, u32[]{:S(2)}) copy-start(bf16[9,2,16,4096]{3,2,1,0:T(8,128)(2,1)} %param.31) | copy-start | bytes 7077892
  161.8 40.8 %all-to-all-start.1 = ((bf16[9,2,16,16,256]{4,2,1,0,3:T(8,128)(2,1)}), bf16[9,2,16,16,256]{4,2,1,0,3:T(8,128)(2,1)S(1)}, u32[]{:S(2)}, u32[]{:S(2)}) async-start(bf16[9,2,16,16,256]{4,2,1,0,3:T(8,128)(2,1)} %bitcast.69), calls=%async_computation.1 | async-start | bytes 4718592 | tf_op jit(solution)/shard_map/all_to_all | solution.py:73
  172.1 3.3 copy-start.16
  172.1 138.5 %reduce-scatter.5.cloned.1.call-start = ((), (), s32[]{:S(2)}) async-start(), calls=%async_computation.7 | async-start | bytes 2228224 | tf_op jit(solution)/shard_map/reduce_scatter | solution.py:147
  206.6 2.2 copy-start.5
  208.9 10.2 %copy-start.6 = (bf16[512,2,128]{0,2,1:T(8,128)(2,1)S(1)}, bf16[512,2,128]{0,2,1:T(8,128)(2,1)}, u32[]{:S(2)}) copy-start(bf16[512,2,128]{0,2,1:T(8,128)(2,1)} %fusion.122) | copy-start | bytes 786436
  225.0 6.3 %copy-start.3 = (f32[256,4096]{1,0:T(8,128)S(1)}, f32[256,4096]{1,0:T(8,128)}, u32[]{:S(2)}) copy-start(f32[256,4096]{1,0:T(8,128)} %fusion.54) | copy-start | bytes 12582916
  228.1 3.2 copy-start.1
  231.3 1.9 slice-start
  233.2 142.2 %copy-start.13 = (f32[256]{0:T(256)S(1)}, f32[256]{0:T(256)}, u32[]{:S(2)}) copy-start(f32[256]{0:T(256)} %param.30) | copy-start | bytes 3076
  233.2 142.2 %copy-start.14 = (f32[256]{0:T(256)S(1)}, f32[256]{0:T(256)}, u32[]{:S(2)}) copy-start(f32[256]{0:T(256)} %param.26) | copy-start | bytes 3076
  248.3 127.0 %reduce-scatter.3.cloned.1.call-start = ((), (), s32[]{:S(2)}) async-start(), calls=%async_computation.6 | async-start | bytes 2228224 | tf_op jit(solution)/shard_map/reduce_scatter | solution.py:145
Sparse Core Ops, SparseCore 0:
  18.7 131.0 all-gather.1
  248.4 62.0 reduce-scatter.4
  312.9 62.3 reduce-scatter.2
